TPU v7x, 32 devices: a whole 2x2x4 slice. The times are simulated.
32 devices in a mesh: blk: 8 (over y, x, core), xfer: 4 (over z).
Axes of the slice: x: 2, y: 2, z: 4, core: 2. Of those that a mesh axis runs over, the one named last changes fastest.
Arguments:
- greens: bfloat16 [8, 2, 256, 256], P('blk'), may hold values from -6 to 6
- transfer_index: int32 [64, 256], P(('blk', 'xfer')), may hold values from 0 to 255, as said below
- phase_index: int32 [64, 256], P(('blk', 'xfer')), may hold values from 0 to 7
- partner_slot: int32 [64], P(('blk', 'xfer')), may hold values from 0 to 1, as said below
- conj_index: int32 [256], replicated, may hold values from 0 to 255, as said below
Outputs:
- four_point: float32 [64, 2, 256, 256], P(('blk', 'xfer'))
Inputs may be any that keep to these rules, and one draw needn't show every extreme that they name: `transfer_index`: each row is a permutation: the momentum-frequency shifted by the row's transfer, momenta on a periodic 4 x 4 cluster and frequencies cyclic over 16. `conj_index`: an involution: the index of the negated momentum and the mirrored frequency. `partner_slot`: the pairing is mutual: if transfer q in slot s has partner slot t on the partner device, the transfer in slot t there has partner slot s.
All inputs are finite; a program needn't handle non-finite values.
Results may differ from a plain program's by a relative error of at most 0.0003.
Values may be sent and summed in bfloat16 or wider, within the bound.
No kernel may reach another device: no remote copies, remote signals or barrier semaphores. Data moves between devices by JAX's collectives and lax.ppermute only.
A program may use at most 64 MiB of HBM per device.

v0:
```python
import math
import jax
import jax.numpy as jnp
from jax import lax
from jax.sharding import PartitionSpec as P

NPH = 8


def passed_along(value, axis, by):
    size = lax.axis_size(axis)
    return lax.ppermute(value, axis, [(i, (i + by) % size) for i in range(size)])


def rotations(phase_rows):
    angle = (
        2.0 * math.pi / NPH * (phase_rows[:, :, None] - phase_rows[:, None, :]).astype(jnp.float32)
    )
    return (jnp.cos(angle), jnp.sin(angle))


def selectors(index_rows, width):
    columns = jnp.arange(width, dtype=jnp.int32)
    return (columns[None, :, None] == index_rows[:, None, :]).astype(jnp.bfloat16)


def turned(total, cosines, sines):
    real = cosines * total[:, 0] - sines * total[:, 1]
    imag = cosines * total[:, 1] + sines * total[:, 0]
    return jnp.stack([real, imag], axis=1)


def mirrored(slices, conj_index):
    flipped = jnp.swapaxes(jnp.take(jnp.take(slices, conj_index, axis=2), conj_index, axis=3), 2, 3)
    return jnp.stack([flipped[:, 0], -flipped[:, 1]], axis=1)


def crossed(total, block, index_rows, picking):
    flipped = jnp.swapaxes(block, 1, 2)
    chosen = jnp.take(flipped, index_rows, axis=1)
    moved = jnp.einsum("csaj,sjb->csab", chosen, picking, preferred_element_type=jnp.float32)
    block_real = block[0].astype(jnp.float32)
    block_imag = block[1].astype(jnp.float32)
    real = block_real * moved[0] - block_imag * moved[1]
    imag = block_real * moved[1] + block_imag * moved[0]
    return total + jnp.stack([real, imag], axis=1)


def local(greens, transfer_index, phase_index, partner_slot, conj_index):
    slots = transfer_index.shape[0]
    width = greens.shape[-1]
    blocks = lax.axis_size("blk")
    groups = lax.axis_size("xfer")
    halfway = groups // 2
    scale = 0.5 / math.sqrt(blocks)
    cosines, sines = rotations(phase_index)
    picking = selectors(transfer_index, width)
    empty = jnp.zeros((slots, 2, width, width), jnp.float32)

    def visit(running, block):
        return (crossed(running, block, transfer_index, picking), None)

    sums = lax.scan(visit, empty, lax.all_gather(greens, "blk", axis=0, tiled=True))[0]
    sums = turned(sums, cosines, sines)
    partner = passed_along(sums, "xfer", halfway)
    mirror = jnp.take(partner, partner_slot, axis=0)
    return (sums + mirrored(mirror, conj_index)) * scale


def solution(mesh):
    in_specs = (
        P("blk", None, None, None),
        P(("blk", "xfer"), None),
        P(("blk", "xfer"), None),
        P(("blk", "xfer")),
        P(),
    )
    out_specs = P(("blk", "xfer"), None, None, None)
    return jax.shard_map(local, mesh=mesh, in_specs=in_specs, out_specs=out_specs, check_vma=False)
```

profile of v0, /device:TPU:0, one launch (start us, length us, event | category | flops | bytes accessed | tf_op | source)
XLA Modules:
  0.0 156.7 jit_solution(5556600198563763163)
XLA Ops:
  7.3 32.6 %all-gather.2.cloned.1.call-done = bf16[8,2,256,256]{3,2,1,0:T(8,128)(2,1)} async-done(((bf16[1,2,256,256]{3,2,1,0:T(8,128)(2,1)}), bf16[8,2,256,256]{3,2,1,0:T(8,128)(2,1)}) %all-gather.2.cloned.1.call-update) | async-done | bytes 2097168 | tf_op jit(solution)/shard_map/all_gather | solution.py:63
  39.9 51.2 %while.13 = (s32[]{:T(128)}, f32[2,2,256,256]{3,2,0,1:T(8,128)S(1)}, bf16[8,2,256,256]{3,2,1,0:T(8,128)(2,1)}, s32[2,256]{1,0:T(2,128)}, s32[]{:T(128)}, /*index=5*/s32[]{:T(128)}, s32[]{}) while((s32[]{:T(128)}, f32[2,2,256,256]{3,2,0,1:T(8,128)S(1)}, bf16[8,2,256,256]{3,2,1,0:T(8,128)(2,1)}, ...), condition=%wide.region_1.2_spmd.clone.clone.clone, body=%wide.region_0.1_spmd.clone.clone.clone.sunk | while | flops 136451584 | bytes 11302027 | solution.py:63
  41.8 2.6 %gather_fusion = bf16[512,2,256]{2,1,0:T(2,128)(2,1)S(1)} fusion(bf16[2,256,256]{2,0,1:T(2,128)(2,1)S(1)} %bitcast.71, s32[1024]{0:T(1024)S(1)} %pad_clamp_fusion.4), kind=kCustom, calls=%fused_computation.clone.clone.clone.clone.1 | custom fusion | bytes 1050624 | tf_op jit(solution)/shard_map/while/body/eval_jaxpr/jit(_take)/gather | solution.py:40
  44.8 1.0 fusion.24
  48.2 2.6 %gather_fusion = bf16[512,2,256]{2,1,0:T(2,128)(2,1)S(1)} fusion(bf16[2,256,256]{2,0,1:T(2,128)(2,1)S(1)} %bitcast.71, s32[1024]{0:T(1024)S(1)} %pad_clamp_fusion.4), kind=kCustom, calls=%fused_computation.clone.clone.clone.clone.1 | custom fusion | bytes 1050624 | tf_op jit(solution)/shard_map/while/body/eval_jaxpr/jit(_take)/gather | solution.py:40
  51.2 1.0 fusion.24
  54.6 2.6 %gather_fusion = bf16[512,2,256]{2,1,0:T(2,128)(2,1)S(1)} fusion(bf16[2,256,256]{2,0,1:T(2,128)(2,1)S(1)} %bitcast.71, s32[1024]{0:T(1024)S(1)} %pad_clamp_fusion.4), kind=kCustom, calls=%fused_computation.clone.clone.clone.clone.1 | custom fusion | bytes 1050624 | tf_op jit(solution)/shard_map/while/body/eval_jaxpr/jit(_take)/gather | solution.py:40
  57.6 1.0 fusion.24
  61.0 2.6 %gather_fusion = bf16[512,2,256]{2,1,0:T(2,128)(2,1)S(1)} fusion(bf16[2,256,256]{2,0,1:T(2,128)(2,1)S(1)} %bitcast.71, s32[1024]{0:T(1024)S(1)} %pad_clamp_fusion.4), kind=kCustom, calls=%fused_computation.clone.clone.clone.clone.1 | custom fusion | bytes 1050624 | tf_op jit(solution)/shard_map/while/body/eval_jaxpr/jit(_take)/gather | solution.py:40
  64.0 1.0 fusion.24
  67.4 2.6 %gather_fusion = bf16[512,2,256]{2,1,0:T(2,128)(2,1)S(1)} fusion(bf16[2,256,256]{2,0,1:T(2,128)(2,1)S(1)} %bitcast.71, s32[1024]{0:T(1024)S(1)} %pad_clamp_fusion.4), kind=kCustom, calls=%fused_computation.clone.clone.clone.clone.1 | custom fusion | bytes 1050624 | tf_op jit(solution)/shard_map/while/body/eval_jaxpr/jit(_take)/gather | solution.py:40
  70.4 1.0 fusion.24
  73.8 2.6 %gather_fusion = bf16[512,2,256]{2,1,0:T(2,128)(2,1)S(1)} fusion(bf16[2,256,256]{2,0,1:T(2,128)(2,1)S(1)} %bitcast.71, s32[1024]{0:T(1024)S(1)} %pad_clamp_fusion.4), kind=kCustom, calls=%fused_computation.clone.clone.clone.clone.1 | custom fusion | bytes 1050624 | tf_op jit(solution)/shard_map/while/body/eval_jaxpr/jit(_take)/gather | solution.py:40
  76.8 1.0 fusion.24
  80.2 2.6 %gather_fusion = bf16[512,2,256]{2,1,0:T(2,128)(2,1)S(1)} fusion(bf16[2,256,256]{2,0,1:T(2,128)(2,1)S(1)} %bitcast.71, s32[1024]{0:T(1024)S(1)} %pad_clamp_fusion.4), kind=kCustom, calls=%fused_computation.clone.clone.clone.clone.1 | custom fusion | bytes 1050624 | tf_op jit(solution)/shard_map/while/body/eval_jaxpr/jit(_take)/gather | solution.py:40
  83.2 1.0 fusion.24
  86.6 2.6 %gather_fusion = bf16[512,2,256]{2,1,0:T(2,128)(2,1)S(1)} fusion(bf16[2,256,256]{2,0,1:T(2,128)(2,1)S(1)} %bitcast.71, s32[1024]{0:T(1024)S(1)} %pad_clamp_fusion.4), kind=kCustom, calls=%fused_computation.clone.clone.clone.clone.1 | custom fusion | bytes 1050624 | tf_op jit(solution)/shard_map/while/body/eval_jaxpr/jit(_take)/gather | solution.py:40
  89.6 1.0 fusion.24
  91.2 2.0 %multiply_subtract_fusion.1 = (f32[2,1,256,256]{3,2,1,0:T(8,128)S(1)}, f32[2,1,256,256]{3,2,1,0:T(8,128)S(1)}) fusion(s32[2,256]{1,0:T(2,128)S(1)} %copy-done.1, f32[2,2,256,256]{3,2,0,1:T(8,128)S(1)} %get-tuple-element.32), kind=kLoop, calls=%fused_computation.37 | loop fusion | flops 1179648 | bytes 2101248 | tf_op jit(solution)/shard_map/sub | solution.py:28
  93.3 2.5 %collective-permute-start = (f32[2,2,256,256]{3,2,1,0:T(8,128)S(1)}, f32[2,2,256,256]{3,2,1,0:T(8,128)S(1)}, u32[]{:S(2)}, u32[]{:S(2)}) collective-permute-start(f32[2,2,256,256]{3,2,1,0:T(8,128)S(1)} %pad_maximum_fusion), channel_id=1, source_target_pairs={{0,2},{1,3},{2,0},{3,1},{4,6},{5,7},{6,4},{7,5},{8,10},{9,11},{10,... | collective-permute-start | bytes 3145736 | tf_op jit(solution)/shard_map/ppermute | solution.py:12
  95.9 46.2 %collective-permute-done = f32[2,2,256,256]{3,2,1,0:T(8,128)S(1)} collective-permute-done((f32[2,2,256,256]{3,2,1,0:T(8,128)S(1)}, f32[2,2,256,256]{3,2,1,0:T(8,128)S(1)}, u32[]{:S(2)}, u32[]{:S(2)}) %collective-permute-start) | collective-permute-done | bytes 1048608 | tf_op jit(solution)/shard_map/ppermute | solution.py:12
  143.7 1.9 %gather_fusion.2 = f32[256,2,2,256]{3,2,1,0:T(2,128)S(1)} fusion(f32[2,2,256,256]{3,1,2,0:T(2,128)S(1)} %copy.34, s32[1024]{0:T(1024)S(1)} %pad_clamp_fusion.1), kind=kCustom, calls=%fused_computation.2 | custom fusion | bytes 2098176 | tf_op jit(solution)/shard_map/jit(_take)/gather | solution.py:34
  146.4 1.9 %gather_fusion.3 = f32[256,2,2,256]{3,2,1,0:T(2,128)S(1)} fusion(f32[2,2,256,256]{2,1,3,0:T(2,128)S(1)} %copy.36, s32[1024]{0:T(1024)S(1)} %pad_clamp_fusion.1), kind=kCustom, calls=%fused_computation.3 | custom fusion | bytes 2098176 | tf_op jit(solution)/shard_map/jit(_take)/gather | solution.py:34
  148.7 1.1 fusion.10
  (119 shorter events, 25.5 us)
Async XLA Ops:
  6.5 33.3 %all-gather.2.cloned.1.call-start = ((), (), s32[]{:S(2)}) async-start(), calls=%async_computation | async-start | bytes 2359296 | tf_op jit(solution)/shard_map/all_gather | solution.py:63
  39.9 51.3 %copy-start.1 = (s32[2,256]{1,0:T(2,128)S(1)}, s32[2,256]{1,0:T(2,128)}, u32[]{:S(2)}) copy-start(s32[2,256]{1,0:T(2,128)} %param.9) | copy-start | bytes 6148
  39.9 4.5 %copy-start = (s32[2,256]{1,0:T(2,128)S(1)}, s32[2,256]{1,0:T(2,128)}, u32[]{:S(2)}) copy-start(s32[2,256]{1,0:T(2,128)} %get-tuple-element.146) | copy-start | bytes 6148 | tf_op jit(solution)/shard_map/while
  46.3 4.5 %copy-start = (s32[2,256]{1,0:T(2,128)S(1)}, s32[2,256]{1,0:T(2,128)}, u32[]{:S(2)}) copy-start(s32[2,256]{1,0:T(2,128)} %get-tuple-element.146) | copy-start | bytes 6148 | tf_op jit(solution)/shard_map/while
  52.7 4.5 %copy-start = (s32[2,256]{1,0:T(2,128)S(1)}, s32[2,256]{1,0:T(2,128)}, u32[]{:S(2)}) copy-start(s32[2,256]{1,0:T(2,128)} %get-tuple-element.146) | copy-start | bytes 6148 | tf_op jit(solution)/shard_map/while
  59.1 4.5 %copy-start = (s32[2,256]{1,0:T(2,128)S(1)}, s32[2,256]{1,0:T(2,128)}, u32[]{:S(2)}) copy-start(s32[2,256]{1,0:T(2,128)} %get-tuple-element.146) | copy-start | bytes 6148 | tf_op jit(solution)/shard_map/while
  65.5 4.5 %copy-start = (s32[2,256]{1,0:T(2,128)S(1)}, s32[2,256]{1,0:T(2,128)}, u32[]{:S(2)}) copy-start(s32[2,256]{1,0:T(2,128)} %get-tuple-element.146) | copy-start | bytes 6148 | tf_op jit(solution)/shard_map/while
  71.9 4.5 %copy-start = (s32[2,256]{1,0:T(2,128)S(1)}, s32[2,256]{1,0:T(2,128)}, u32[]{:S(2)}) copy-start(s32[2,256]{1,0:T(2,128)} %get-tuple-element.146) | copy-start | bytes 6148 | tf_op jit(solution)/shard_map/while
  78.3 4.5 %copy-start = (s32[2,256]{1,0:T(2,128)S(1)}, s32[2,256]{1,0:T(2,128)}, u32[]{:S(2)}) copy-start(s32[2,256]{1,0:T(2,128)} %get-tuple-element.146) | copy-start | bytes 6148 | tf_op jit(solution)/shard_map/while
  84.7 4.5 %copy-start = (s32[2,256]{1,0:T(2,128)S(1)}, s32[2,256]{1,0:T(2,128)}, u32[]{:S(2)}) copy-start(s32[2,256]{1,0:T(2,128)} %get-tuple-element.146) | copy-start | bytes 6148 | tf_op jit(solution)/shard_map/while
  91.1 4.7 %copy-start.3 = (s32[2]{0:T(128)S(1)}, s32[2]{0:T(128)}, u32[]{:S(2)}) copy-start(s32[2]{0:T(128)} %param.10) | copy-start | bytes 28
  91.1 4.7 %copy-start.2 = (s32[256]{0:T(256)S(1)}, s32[256]{0:T(256)}, u32[]{:S(2)}) copy-start(s32[256]{0:T(256)} %param.11) | copy-start | bytes 3076
  93.3 48.8 %collective-permute-start = (f32[2,2,256,256]{3,2,1,0:T(8,128)S(1)}, f32[2,2,256,256]{3,2,1,0:T(8,128)S(1)}, u32[]{:S(2)}, u32[]{:S(2)}) collective-permute-start(f32[2,2,256,256]{3,2,1,0:T(8,128)S(1)} %pad_maximum_fusion), channel_id=1, source_target_pairs={{0,2},{1,3},{2,0},{3,1},{4,6},{5,7},{6,4},{7,5},{8,10},{9,11},{10,... | collective-permute-start | bytes 3145736 | tf_op jit(solution)/shard_map/ppermute | solution.py:12
Sparse Core Ops, SparseCore 0:
  9.2 30.5 all-gather.1
where the time goes:
time: 157 us
  waiting for transfers between devices  79.5 us (51%)
  local copies, waits for them, and re-layouts  36.2 us (23%)
  other arithmetic  21.3 us (14%)
  between operations  13.5 us (9%)
  matrix products  2.84 us (2%)
  starting transfers between devices  2.48 us (2%)
    ppermute x1, waiting for transfers between devices, passed_along(): lax.ppermute(value, axis, [(i, (i + by) % size) for i in range(size)])  46.2 us
    all_gather x1, waiting for transfers between devices, local(): lax.all_gather(greens, 'blk', axis=0, tiled=True)  32.6 us
    gather x16, local copies, waits for them, and re-layouts, crossed(): chosen = jnp.take(flipped, index_rows, axis=1)  21.1 us
    dynamic_slice x16, local copies, waits for them, and re-layouts, local(): lax.scan(visit, empty, lax.all_gather(greens, 'blk', axis=0, tiled=True))[0]  9.24 us
    convert_element_type x8, other arithmetic, crossed(): block_real = block[0].astype(jnp.float32)  8.09 us
    while x8, other arithmetic  5.49 us
  transfers between devices with their start and end apart: 2, of which 2 were waited for; matrix products, arithmetic and copies ran while one was open for 0% of the time, Pallas kernels for 0%

commit v1 on v0

--- a/solution.py
+++ b/solution.py
@@ -5,6 +5,22 @@
 from jax.sharding import PartitionSpec as P
 
 NPH = 8
+
+
+def gather_around(x, axis, dim):
+    ways, here, step = (lax.axis_size(axis), lax.axis_index(axis), x.shape[dim])
+    shape = [n * ways if d == dim else n for d, n in enumerate(x.shape)]
+    full = lax.dynamic_update_slice_in_dim(jnp.zeros(shape, x.dtype), x, here * step, axis=dim)
+    going_up = going_down = x
+    for far in range(1, ways // 2 + 1):
+        going_up = lax.ppermute(going_up, axis, [(d, (d + 1) % ways) for d in range(ways)])
+        full = lax.dynamic_update_slice_in_dim(full, going_up, (here - far) % ways * step, axis=dim)
+        if 2 * far < ways:
+            going_down = lax.ppermute(going_down, axis, [(d, (d - 1) % ways) for d in range(ways)])
+            full = lax.dynamic_update_slice_in_dim(
+                full, going_down, (here + far) % ways * step, axis=dim
+            )
+    return full
 
 
 def passed_along(value, axis, by):
@@ -60,7 +76,7 @@
     def visit(running, block):
         return (crossed(running, block, transfer_index, picking), None)
 
-    sums = lax.scan(visit, empty, lax.all_gather(greens, "blk", axis=0, tiled=True))[0]
+    sums = lax.scan(visit, empty, gather_around(greens, "blk", 0))[0]
     sums = turned(sums, cosines, sines)
     partner = passed_along(sums, "xfer", halfway)
     mirror = jnp.take(partner, partner_slot, axis=0)

time: 157 us -> 134 us (0.85)
  waiting for transfers between devices: 79.5 us -> 53.8 us
  starting transfers between devices: 2.48 us -> 16.8 us
  between operations: 13.5 us -> 0.17 us
  local copies, waits for them, and re-layouts: 36.2 us -> 43.4 us
  other arithmetic: 21.3 us -> 15.8 us
    all_gather x1 -> x0, waiting for transfers between devices: 32.6 us -> none  [local(): lax.all_gather(greens, 'blk', axis=0, tiled=True)]
    ppermute x0 -> x7, waiting for transfers between devices: none -> 12.2 us  [the longest x4 10.4 us: gather_around(): lax.ppermute(going_up, axis, [(d, (d + 1) % ways) for d in range(ways)])]
    ppermute x0 -> x7, starting transfers between devices: none -> 9.56 us  [the longest x3 8.44 us: gather_around(): lax.ppermute(going_down, axis, [(d, (d - 1) % ways) for d in range(ways)])]
    dynamic_update_slice x0 -> x8, local copies, waits for them, and re-layouts: none -> 5.78 us  [the longest x4 2.92 us: gather_around(): lax.dynamic_update_slice_in_dim(full, going_up, (here - far) % ways * ste...]
    while x8, other arithmetic: 5.49 us -> 0.03 us
    ppermute x1, starting transfers between devices: 2.48 us -> 7.21 us  [passed_along(): lax.ppermute(value, axis, [(i, (i + by) % size) for i in range(size)])]
    ppermute x1, waiting for transfers between devices: 46.2 us -> 41.7 us  [passed_along(): lax.ppermute(value, axis, [(i, (i + by) % size) for i in range(size)])]
  transfers between devices with their start and end apart: 2 -> 8, of which waited for: 2 -> 8; matrix products, arithmetic and copies ran while one was open for 0% -> 5% of each run, Pallas kernels for 0% -> 0%
where the time goes in v1:
time: 134 us
  waiting for transfers between devices  53.8 us (40%)
  local copies, waits for them, and re-layouts  43.4 us (32%)
  starting transfers between devices  16.8 us (13%)
  other arithmetic  15.8 us (12%)
  matrix products  2.84 us (2%)
    ppermute x1, waiting for transfers between devices, passed_along(): lax.ppermute(value, axis, [(i, (i + by) % size) for i in range(size)])  41.7 us
    gather x16, local copies, waits for them, and re-layouts, crossed(): chosen = jnp.take(flipped, index_rows, axis=1)  21.1 us
    ppermute x4, waiting for transfers between devices, gather_around(): lax.ppermute(going_up, axis, [(d, (d + 1) % ways) for d in range(ways)])  10.4 us
    dynamic_slice x16, local copies, waits for them, and re-layouts, local(): sums = lax.scan(visit, empty, gather_around(greens, 'blk', 0))[0]  9.21 us
    ppermute x3, starting transfers between devices, gather_around(): lax.ppermute(going_down, axis, [(d, (d - 1) % ways) for d in range(ways)])  8.44 us
    convert_element_type x8, other arithmetic, crossed(): block_real = block[0].astype(jnp.float32)  8.09 us
    ppermute x1, starting transfers between devices, passed_along(): lax.ppermute(value, axis, [(i, (i + by) % size) for i in range(size)])  7.21 us
    dynamic_update_slice x4, local copies, waits for them, and re-layouts, gather_around(): lax.dynamic_update_slice_in_dim(full, going_up, (here - far) % ways * ste...  2.92 us
  transfers between devices with their start and end apart: 8, of which 8 were waited for; matrix products, arithmetic and copies ran while one was open for 5% of the time, Pallas kernels for 0%

profile of v1, /device:TPU:0, one launch (start us, length us, event | category | flops | bytes accessed | tf_op | source)
XLA Modules:
  0.0 133.7 jit_solution(9105344702761095299)
XLA Ops:
  0.5 2.9 %collective-permute-start.1 = (bf16[1,2,256,256]{3,2,1,0:T(8,128)(2,1)}, bf16[1,2,256,256]{3,2,1,0:T(8,128)(2,1)S(1)}, u32[]{:S(2)}, u32[]{:S(2)}) collective-permute-start(bf16[1,2,256,256]{3,2,1,0:T(8,128)(2,1)} %param.7), channel_id=1, source_target_pairs={{0,28},{4,0},{8,4},{12,8},{16,12},{20,16},{24,20},{28,24},{1,29},{... | collective-permute-start | bytes 786440 | tf_op jit(solution)/shard_map/ppermute | solution.py:19
  3.4 4.5 %collective-permute-done = bf16[1,2,256,256]{3,2,1,0:T(8,128)(2,1)S(1)} collective-permute-done((bf16[1,2,256,256]{3,2,1,0:T(8,128)(2,1)}, bf16[1,2,256,256]{3,2,1,0:T(8,128)(2,1)S(1)}, u32[]{:S(2)}, u32[]{:S(2)}) %collective-permute-start) | collective-permute-done | bytes 262176 | tf_op jit(solution)/shard_map/ppermute | solution.py:16
  9.4 2.7 %collective-permute-start.3 = (bf16[1,2,256,256]{3,2,1,0:T(8,128)(2,1)S(1)}, bf16[1,2,256,256]{3,2,1,0:T(8,128)(2,1)S(1)}, u32[]{:S(2)}, u32[]{:S(2)}) collective-permute-start(bf16[1,2,256,256]{3,2,1,0:T(8,128)(2,1)S(1)} %collective-permute-done.1), channel_id=1, source_target_pairs={{0,28},{4,0},{8,4},{12,8},{16,12},{20,16},{24,20},{28,24},{1,29},{... | collective-permute-start | bytes 786440 | tf_op jit(solution)/shard_map/ppermute | solution.py:19
  12.1 1.5 %broadcast_in_dim.55 = bf16[8,2,256,256]{3,2,1,0:T(8,128)(2,1)} broadcast(bf16[]{:T(256)} %constant.112.clone.1), dimensions={} | broadcast | bytes 2097154 | tf_op jit(solution)/shard_map/broadcast_in_dim | solution.py:13
  16.9 2.8 %collective-permute-start.5 = (bf16[1,2,256,256]{3,2,1,0:T(8,128)(2,1)S(1)}, bf16[1,2,256,256]{3,2,1,0:T(8,128)(2,1)S(1)}, u32[]{:S(2)}, u32[]{:S(2)}) collective-permute-start(bf16[1,2,256,256]{3,2,1,0:T(8,128)(2,1)S(1)} %collective-permute-done.3), channel_id=1, source_target_pairs={{0,28},{4,0},{8,4},{12,8},{16,12},{20,16},{24,20},{28,24},{1,29},{... | collective-permute-start | bytes 786440 | tf_op jit(solution)/shard_map/ppermute | solution.py:19
  20.4 1.3 collective-permute-done.4
  24.3 4.1 %collective-permute-done.6 = bf16[1,2,256,256]{3,2,1,0:T(8,128)(2,1)S(1)} collective-permute-done((bf16[1,2,256,256]{3,2,1,0:T(8,128)(2,1)S(1)}, bf16[1,2,256,256]{3,2,1,0:T(8,128)(2,1)S(1)}, u32[]{:S(2)}, u32[]{:S(2)}) %collective-permute-start.6) | collective-permute-done | bytes 262176 | tf_op jit(solution)/shard_map/ppermute | solution.py:16
  29.1 45.7 %while.13 = (s32[]{:T(128)}, f32[2,2,256,256]{3,2,0,1:T(8,128)S(1)}, bf16[8,2,256,256]{3,2,1,0:T(8,128)(2,1)}, s32[2,256]{1,0:T(2,128)S(1)}, s32[]{:T(128)}, /*index=5*/s32[]{:T(128)}, s32[]{}) while((s32[]{:T(128)}, f32[2,2,256,256]{3,2,0,1:T(8,128)S(1)}, bf16[8,2,256,256]{3,2,1,0:T(8,128)(2,1)}, ...), condition=%wide.region_1.2_spmd.clone.clone.clone, body=%wide.region_0.1_spmd.clone.clone.clone.sunk | while | flops 136451584 | bytes 11293807 | solution.py:79
  30.3 2.6 %gather_fusion = bf16[512,2,256]{2,1,0:T(2,128)(2,1)S(1)} fusion(bf16[2,256,256]{2,0,1:T(2,128)(2,1)S(1)} %bitcast.71, s32[1024]{0:T(1024)S(1)} %pad_clamp_fusion.4), kind=kCustom, calls=%fused_computation.clone.clone.clone.clone.1 | custom fusion | bytes 1050624 | tf_op jit(solution)/shard_map/while/body/eval_jaxpr/jit(_take)/gather | solution.py:56
  33.3 1.0 fusion.24
  36.0 2.6 %gather_fusion = bf16[512,2,256]{2,1,0:T(2,128)(2,1)S(1)} fusion(bf16[2,256,256]{2,0,1:T(2,128)(2,1)S(1)} %bitcast.71, s32[1024]{0:T(1024)S(1)} %pad_clamp_fusion.4), kind=kCustom, calls=%fused_computation.clone.clone.clone.clone.1 | custom fusion | bytes 1050624 | tf_op jit(solution)/shard_map/while/body/eval_jaxpr/jit(_take)/gather | solution.py:56
  39.1 1.0 fusion.24
  41.7 2.6 %gather_fusion = bf16[512,2,256]{2,1,0:T(2,128)(2,1)S(1)} fusion(bf16[2,256,256]{2,0,1:T(2,128)(2,1)S(1)} %bitcast.71, s32[1024]{0:T(1024)S(1)} %pad_clamp_fusion.4), kind=kCustom, calls=%fused_computation.clone.clone.clone.clone.1 | custom fusion | bytes 1050624 | tf_op jit(solution)/shard_map/while/body/eval_jaxpr/jit(_take)/gather | solution.py:56
  47.5 2.6 %gather_fusion = bf16[512,2,256]{2,1,0:T(2,128)(2,1)S(1)} fusion(bf16[2,256,256]{2,0,1:T(2,128)(2,1)S(1)} %bitcast.71, s32[1024]{0:T(1024)S(1)} %pad_clamp_fusion.4), kind=kCustom, calls=%fused_computation.clone.clone.clone.clone.1 | custom fusion | bytes 1050624 | tf_op jit(solution)/shard_map/while/body/eval_jaxpr/jit(_take)/gather | solution.py:56
  53.2 2.6 %gather_fusion = bf16[512,2,256]{2,1,0:T(2,128)(2,1)S(1)} fusion(bf16[2,256,256]{2,0,1:T(2,128)(2,1)S(1)} %bitcast.71, s32[1024]{0:T(1024)S(1)} %pad_clamp_fusion.4), kind=kCustom, calls=%fused_computation.clone.clone.clone.clone.1 | custom fusion | bytes 1050624 | tf_op jit(solution)/shard_map/while/body/eval_jaxpr/jit(_take)/gather | solution.py:56
  58.9 2.6 %gather_fusion = bf16[512,2,256]{2,1,0:T(2,128)(2,1)S(1)} fusion(bf16[2,256,256]{2,0,1:T(2,128)(2,1)S(1)} %bitcast.71, s32[1024]{0:T(1024)S(1)} %pad_clamp_fusion.4), kind=kCustom, calls=%fused_computation.clone.clone.clone.clone.1 | custom fusion | bytes 1050624 | tf_op jit(solution)/shard_map/while/body/eval_jaxpr/jit(_take)/gather | solution.py:56
  64.6 2.6 %gather_fusion = bf16[512,2,256]{2,1,0:T(2,128)(2,1)S(1)} fusion(bf16[2,256,256]{2,0,1:T(2,128)(2,1)S(1)} %bitcast.71, s32[1024]{0:T(1024)S(1)} %pad_clamp_fusion.4), kind=kCustom, calls=%fused_computation.clone.clone.clone.clone.1 | custom fusion | bytes 1050624 | tf_op jit(solution)/shard_map/while/body/eval_jaxpr/jit(_take)/gather | solution.py:56
  70.3 2.6 %gather_fusion = bf16[512,2,256]{2,1,0:T(2,128)(2,1)S(1)} fusion(bf16[2,256,256]{2,0,1:T(2,128)(2,1)S(1)} %bitcast.71, s32[1024]{0:T(1024)S(1)} %pad_clamp_fusion.4), kind=kCustom, calls=%fused_computation.clone.clone.clone.clone.1 | custom fusion | bytes 1050624 | tf_op jit(solution)/shard_map/while/body/eval_jaxpr/jit(_take)/gather | solution.py:56
  74.9 2.0 %multiply_subtract_fusion.1 = (f32[2,1,256,256]{3,2,1,0:T(8,128)S(1)}, f32[2,1,256,256]{3,2,1,0:T(8,128)S(1)}) fusion(s32[2,256]{1,0:T(2,128)S(1)} %copy-done.2, f32[2,2,256,256]{3,2,0,1:T(8,128)S(1)} %get-tuple-element.32), kind=kLoop, calls=%fused_computation.37 | loop fusion | flops 1179648 | bytes 2101248 | tf_op jit(solution)/shard_map/sub | solution.py:44
  77.0 7.2 %collective-permute-start.7 = (f32[2,2,256,256]{3,2,1,0:T(8,128)S(1)}, f32[2,2,256,256]{3,2,1,0:T(8,128)S(1)}, u32[]{:S(2)}, u32[]{:S(2)}) collective-permute-start(f32[2,2,256,256]{3,2,1,0:T(8,128)S(1)} %pad_maximum_fusion), channel_id=1, source_target_pairs={{0,2},{1,3},{2,0},{3,1},{4,6},{5,7},{6,4},{7,5},{8,10},{9,11},{10,... | collective-permute-start | bytes 3145736 | tf_op jit(solution)/shard_map/ppermute | solution.py:28
  84.3 41.7 %collective-permute-done.7 = f32[2,2,256,256]{3,2,1,0:T(8,128)S(1)} collective-permute-done((f32[2,2,256,256]{3,2,1,0:T(8,128)S(1)}, f32[2,2,256,256]{3,2,1,0:T(8,128)S(1)}, u32[]{:S(2)}, u32[]{:S(2)}) %collective-permute-start.7) | collective-permute-done | bytes 1048608 | tf_op jit(solution)/shard_map/ppermute | solution.py:28
  127.6 1.9 %gather_fusion.2 = f32[256,2,2,256]{3,2,1,0:T(2,128)S(1)} fusion(f32[2,2,256,256]{3,1,2,0:T(2,128)S(1)} %copy.25, s32[1024]{0:T(1024)S(1)} %pad_clamp_fusion.1), kind=kCustom, calls=%fused_computation.2 | custom fusion | bytes 2098176 | tf_op jit(solution)/shard_map/jit(_take)/gather | solution.py:50
  130.3 1.9 %gather_fusion.3 = f32[256,2,2,256]{3,2,1,0:T(2,128)S(1)} fusion(f32[2,2,256,256]{2,1,3,0:T(2,128)S(1)} %copy.27, s32[1024]{0:T(1024)S(1)} %pad_clamp_fusion.1), kind=kCustom, calls=%fused_computation.3 | custom fusion | bytes 2098176 | tf_op jit(solution)/shard_map/jit(_take)/gather | solution.py:50
  132.6 1.1 fusion.10
  (127 shorter events, 34.6 us)
Async XLA Ops:
  0.0 13.6 %copy-start = (bf16[1,2,256,256]{3,2,1,0:T(8,128)(2,1)S(1)}, bf16[1,2,256,256]{3,2,1,0:T(8,128)(2,1)}, u32[]{:S(2)}) copy-start(bf16[1,2,256,256]{3,2,1,0:T(8,128)(2,1)} %param.7) | copy-start | bytes 786436
  0.0 7.9 %collective-permute-start = (bf16[1,2,256,256]{3,2,1,0:T(8,128)(2,1)}, bf16[1,2,256,256]{3,2,1,0:T(8,128)(2,1)S(1)}, u32[]{:S(2)}, u32[]{:S(2)}) collective-permute-start(bf16[1,2,256,256]{3,2,1,0:T(8,128)(2,1)} %param.7), channel_id=1, source_target_pairs={{0,4},{4,8},{8,12},{12,16},{16,20},{20,24},{24,28},{28,0},{1,5},{5... | collective-permute-start | bytes 786440 | tf_op jit(solution)/shard_map/ppermute | solution.py:16
  0.5 8.9 %collective-permute-start.1 = (bf16[1,2,256,256]{3,2,1,0:T(8,128)(2,1)}, bf16[1,2,256,256]{3,2,1,0:T(8,128)(2,1)S(1)}, u32[]{:S(2)}, u32[]{:S(2)}) collective-permute-start(bf16[1,2,256,256]{3,2,1,0:T(8,128)(2,1)} %param.7), channel_id=1, source_target_pairs={{0,28},{4,0},{8,4},{12,8},{16,12},{20,16},{24,20},{28,24},{1,29},{... | collective-permute-start | bytes 786440 | tf_op jit(solution)/shard_map/ppermute | solution.py:19
  7.9 7.0 %collective-permute-start.2 = (bf16[1,2,256,256]{3,2,1,0:T(8,128)(2,1)S(1)}, bf16[1,2,256,256]{3,2,1,0:T(8,128)(2,1)S(1)}, u32[]{:S(2)}, u32[]{:S(2)}) collective-permute-start(bf16[1,2,256,256]{3,2,1,0:T(8,128)(2,1)S(1)} %collective-permute-done), channel_id=1, source_target_pairs={{0,4},{4,8},{8,12},{12,16},{16,20},{20,24},{24,28},{28,0},{1,5},{5... | collective-permute-start | bytes 786440 | tf_op jit(solution)/shard_map/ppermute | solution.py:16
  9.4 7.5 %collective-permute-start.3 = (bf16[1,2,256,256]{3,2,1,0:T(8,128)(2,1)S(1)}, bf16[1,2,256,256]{3,2,1,0:T(8,128)(2,1)S(1)}, u32[]{:S(2)}, u32[]{:S(2)}) collective-permute-start(bf16[1,2,256,256]{3,2,1,0:T(8,128)(2,1)S(1)} %collective-permute-done.1), channel_id=1, source_target_pairs={{0,28},{4,0},{8,4},{12,8},{16,12},{20,16},{24,20},{28,24},{1,29},{... | collective-permute-start | bytes 786440 | tf_op jit(solution)/shard_map/ppermute | solution.py:19
  13.6 15.5 %copy-start.1 = (s32[2,256]{1,0:T(2,128)S(1)}, s32[2,256]{1,0:T(2,128)}, u32[]{:S(2)}) copy-start(s32[2,256]{1,0:T(2,128)} %param.8) | copy-start | bytes 6148
  14.9 6.8 %collective-permute-start.4 = (bf16[1,2,256,256]{3,2,1,0:T(8,128)(2,1)S(1)}, bf16[1,2,256,256]{3,2,1,0:T(8,128)(2,1)S(1)}, u32[]{:S(2)}, u32[]{:S(2)}) collective-permute-start(bf16[1,2,256,256]{3,2,1,0:T(8,128)(2,1)S(1)} %collective-permute-done.2), channel_id=1, source_target_pairs={{0,4},{4,8},{8,12},{12,16},{16,20},{20,24},{24,28},{28,0},{1,5},{5... | collective-permute-start | bytes 786440 | tf_op jit(solution)/shard_map/ppermute | solution.py:16
  16.9 6.7 %collective-permute-start.5 = (bf16[1,2,256,256]{3,2,1,0:T(8,128)(2,1)S(1)}, bf16[1,2,256,256]{3,2,1,0:T(8,128)(2,1)S(1)}, u32[]{:S(2)}, u32[]{:S(2)}) collective-permute-start(bf16[1,2,256,256]{3,2,1,0:T(8,128)(2,1)S(1)} %collective-permute-done.3), channel_id=1, source_target_pairs={{0,28},{4,0},{8,4},{12,8},{16,12},{20,16},{24,20},{28,24},{1,29},{... | collective-permute-start | bytes 786440 | tf_op jit(solution)/shard_map/ppermute | solution.py:19
  21.7 6.7 %collective-permute-start.6 = (bf16[1,2,256,256]{3,2,1,0:T(8,128)(2,1)S(1)}, bf16[1,2,256,256]{3,2,1,0:T(8,128)(2,1)S(1)}, u32[]{:S(2)}, u32[]{:S(2)}) collective-permute-start(bf16[1,2,256,256]{3,2,1,0:T(8,128)(2,1)S(1)} %collective-permute-done.4), channel_id=1, source_target_pairs={{0,4},{4,8},{8,12},{12,16},{16,20},{20,24},{24,28},{28,0},{1,5},{5... | collective-permute-start | bytes 786440 | tf_op jit(solution)/shard_map/ppermute | solution.py:16
  29.1 45.8 %copy-start.2 = (s32[2,256]{1,0:T(2,128)S(1)}, s32[2,256]{1,0:T(2,128)}, u32[]{:S(2)}) copy-start(s32[2,256]{1,0:T(2,128)} %param.9) | copy-start | bytes 6148
  74.9 9.4 %copy-start.4 = (s32[2]{0:T(128)S(1)}, s32[2]{0:T(128)}, u32[]{:S(2)}) copy-start(s32[2]{0:T(128)} %param.10) | copy-start | bytes 28
  74.9 9.4 %copy-start.3 = (s32[256]{0:T(256)S(1)}, s32[256]{0:T(256)}, u32[]{:S(2)}) copy-start(s32[256]{0:T(256)} %param.11) | copy-start | bytes 3076
  77.0 49.0 %collective-permute-start.7 = (f32[2,2,256,256]{3,2,1,0:T(8,128)S(1)}, f32[2,2,256,256]{3,2,1,0:T(8,128)S(1)}, u32[]{:S(2)}, u32[]{:S(2)}) collective-permute-start(f32[2,2,256,256]{3,2,1,0:T(8,128)S(1)} %pad_maximum_fusion), channel_id=1, source_target_pairs={{0,2},{1,3},{2,0},{3,1},{4,6},{5,7},{6,4},{7,5},{8,10},{9,11},{10,... | collective-permute-start | bytes 3145736 | tf_op jit(solution)/shard_map/ppermute | solution.py:28
